TPU v7x, 256 devices: a whole 4x4x8 slice. The times are simulated.
256 devices in a mesh: seq: 32 (over x, z), tensor: 8 (over y, core).
Axes of the slice: x: 4, y: 4, z: 8, core: 2. Of those that a mesh axis runs over, the one named last changes fastest.
Arguments:
- queries: bfloat16 [10240, 4096], P('seq', 'tensor'), may hold values from -8 to 8
- key_rows: bfloat16 [10240, 1024], P('seq', 'tensor'), may hold values from -8 to 8
- value_rows: bfloat16 [10240, 1024], P('seq', 'tensor'), may hold values from -6 to 6
- out_weight: bfloat16 [4096, 8192], P('tensor', 'seq'), may hold values from -0.09375 to 0.09375
- residual_in: bfloat16 [10240, 8192], P('seq'), may hold values from -0.1796875 to 0.1796875
- norm_gain: bfloat16 [8192], replicated, may hold values from 0.099609375 to 1.8984375
- prompt_lengths: int32 [18], replicated, may hold values from 1 to 5120, 10240 in all
Outputs:
- normed: bfloat16 [10240, 8192], P('seq')
- cache_keys: bfloat16 [22528, 1024], P('seq', 'tensor')
- cache_values: bfloat16 [22528, 1024], P('seq', 'tensor')
Inputs may be any that keep to these rules, and one draw needn't show every extreme that they name: `prompt_lengths`: the 18 lengths sum to 10240, and the largest is 5120.
All inputs are finite; a program needn't handle non-finite values.
Results may differ from a plain program's by a relative error of at most 0.019.
Values may be sent and summed in bfloat16 or wider, within the bound.
No kernel may reach another device: no remote copies, remote signals or barrier semaphores. Data moves between devices by JAX's collectives and lax.ppermute only.
A program may use at most 192 MiB of HBM per device.

v0:
```python
import math
import jax
import jax.numpy as jnp
from jax import lax
from jax.sharding import PartitionSpec as P

HD = 128
PAGE = 128
SLOT_DEV = 704


def position_of(stored, per_device, devices):
    half_block = per_device // 2
    device = stored // per_device
    offset = stored % per_device
    return jnp.where(
        offset < half_block,
        device * half_block + offset,
        (2 * devices - 1 - device) * half_block + offset - half_block,
    )


def stored_row(position, per_device, devices):
    half_block = per_device // 2
    block_index = position // half_block
    device = jnp.where(block_index < devices, block_index, 2 * devices - 1 - block_index)
    offset = position % half_block + jnp.where(block_index < devices, 0, half_block)
    return device * per_device + offset


def segment_of(position, lengths):
    doc_ends = jnp.cumsum(lengths, dtype=jnp.int32)
    return jnp.sum(
        (position[:, None] >= doc_ends[None, :]).astype(jnp.int32), axis=1, dtype=jnp.int32
    )


def slot_source(slot_ids, lengths, page_size):
    padded = (lengths + page_size - 1) // page_size * page_size
    page_ends = jnp.cumsum(padded, dtype=jnp.int32)
    page_starts = page_ends - padded
    doc_ends = jnp.cumsum(lengths, dtype=jnp.int32)
    doc_starts = doc_ends - lengths
    before = (slot_ids[:, None] >= page_ends[None, :]).astype(jnp.int32)
    inside = (slot_ids[:, None] >= page_starts[None, :]).astype(jnp.int32) - before
    page_start = jnp.sum(before * padded[None, :], axis=1, dtype=jnp.int32)
    doc_start = jnp.sum(before * lengths[None, :], axis=1, dtype=jnp.int32)
    length = jnp.sum(inside * lengths[None, :], axis=1, dtype=jnp.int32)
    within = slot_ids - page_start
    is_live = within < length
    return (doc_start + within, is_live)


def body(queries, key_rows, value_rows, out_weight, residual_in, norm_gain, prompt_lengths):
    seq_count = lax.axis_size("seq")
    seq_index = lax.axis_index("seq")
    per_device = queries.shape[0]
    kv_local = key_rows.shape[1] // HD
    group_size = queries.shape[1] // (kv_local * HD)
    score_scale = 1.0 / math.sqrt(HD)
    local_rows = jnp.arange(per_device, dtype=jnp.int32) + seq_index * per_device
    my_position = position_of(local_rows, per_device, seq_count)
    my_segment = segment_of(my_position, prompt_lengths)
    grouped = queries.reshape(per_device, kv_local, group_size, HD)
    kv_width = key_rows.shape[1]
    kv_piece = lax.all_gather(
        jnp.concatenate([key_rows, value_rows], axis=1), "seq", axis=0, tiled=True
    )
    key_piece = kv_piece[:, :kv_width]
    value_piece = kv_piece[:, kv_width:]
    piece_rows = key_piece.shape[0]
    key_position = position_of(jnp.arange(piece_rows, dtype=jnp.int32), per_device, seq_count)
    key_segment = segment_of(key_position, prompt_lengths)
    allowed = (key_position[None, :] <= my_position[:, None]) & (
        key_segment[None, :] == my_segment[:, None]
    )
    top_old = jnp.full((kv_local, group_size, per_device), -1e30, jnp.float32)
    scores = (
        jnp.einsum(
            "qgjd,kgd->gjqk",
            grouped,
            key_piece.reshape(piece_rows, kv_local, HD),
            preferred_element_type=jnp.float32,
        )
        * score_scale
    )
    scores = jnp.where(allowed, scores, -1e30)
    top_new = jnp.maximum(top_old, jnp.max(scores, axis=-1))
    weights = jnp.where(allowed, jnp.exp(scores - top_new[..., None]), 0.0)
    total_new = jnp.sum(weights, axis=-1)
    accum_new = jnp.einsum(
        "gjqk,kgd->gjqd",
        weights.astype(jnp.bfloat16),
        value_piece.reshape(piece_rows, kv_local, HD),
        preferred_element_type=jnp.float32,
    )
    attended = jnp.transpose(accum_new / total_new[..., None], (2, 0, 1, 3))
    attended = attended.reshape(per_device, -1).astype(jnp.bfloat16)
    partial_value = jnp.dot(
        attended,
        lax.all_gather(out_weight, "seq", axis=1, tiled=True),
        preferred_element_type=jnp.float32,
    )
    projected = lax.psum(partial_value.astype(jnp.bfloat16), "tensor").astype(jnp.float32)
    hidden = residual_in.astype(jnp.float32) + projected
    mean_square = jnp.mean(hidden * hidden, axis=-1, keepdims=True)
    normed = (hidden * lax.rsqrt(mean_square + 1e-05) * norm_gain.astype(jnp.float32)).astype(
        jnp.bfloat16
    )
    slot_ids = seq_index * SLOT_DEV + jnp.arange(SLOT_DEV, dtype=jnp.int32)
    source, is_live = slot_source(slot_ids, prompt_lengths, PAGE)
    target = stored_row(source, per_device, seq_count)
    empty_cache = jnp.zeros((SLOT_DEV, kv_local * HD), jnp.bfloat16)
    found = is_live & (target >= 0) & (target < piece_rows)
    safe_index = jnp.clip(target, 0, piece_rows - 1)
    cache_keys = jnp.where(found[:, None], jnp.take(key_piece, safe_index, axis=0), empty_cache)
    cache_values = jnp.where(found[:, None], jnp.take(value_piece, safe_index, axis=0), empty_cache)
    return (normed, cache_keys, cache_values)


def solution(mesh):
    return jax.shard_map(
        body,
        mesh=mesh,
        in_specs=(
            P("seq", "tensor"),
            P("seq", "tensor"),
            P("seq", "tensor"),
            P("tensor", "seq"),
            P("seq", None),
            P(),
            P(),
        ),
        out_specs=(P("seq", None), P("seq", "tensor"), P("seq", "tensor")),
        check_vma=False,
    )
```

profile of v0, /device:TPU:1, one launch (start us, length us, event | category | flops | bytes accessed | tf_op | source)
XLA Modules:
  0.0 310.1 jit_solution(13555092218789178911)
XLA Ops:
  7.2 0.0 all-gather.3.cloned.1.call-start
  7.2 1.6 pad_maximum_fusion
  8.9 0.0 all-gather.3.cloned.1.call-update
  8.9 0.0 all-gather.5.cloned.1.call-start
  9.0 0.7 all-gather.5.cloned.1.call-update
  9.7 0.0 all-reduce.2.cloned.1.call-start
  9.7 0.7 copy.17
  10.5 0.1 reduce.2
  10.6 0.7 convert_element_type.52
  11.3 0.7 fusion.65
  12.0 0.1 copy.20
  12.1 0.1 reduce.3
  12.3 0.7 fusion.55
  13.0 0.7 fusion.64
  13.6 0.8 fusion.36
  14.5 0.1 convert_reduce_fusion.1
  14.6 0.2 convert_reduce_fusion
  14.8 4.6 %compare_and_fusion = pred[320,10240]{1,0:T(8,128)(4,1)} fusion(s32[10240]{0:T(1024)S(1)} %convert_reduce_fusion, s32[10240]{0:T(1024)S(1)} %fusion.43, s32[320]{0:T(512)S(1)} %convert_reduce_fusion.1, s32[320]{0:T(512)S(1)} %add_select_fusion.5), kind=kLoop, calls=%fused_computation.10 | loop fusion | flops 9830400 | bytes 3361280 | tf_op jit(solution)/shard_map/and | solution.py:74
  19.4 78.3 %all-gather.3.cloned.1.call-done = bf16[10240,256]{1,0:T(8,128)(2,1)} async-done(((bf16[320,256]{1,0:T(8,128)(2,1)}), bf16[10240,256]{1,0:T(8,128)(2,1)}) %all-gather.3.cloned.1.call-update) | async-done | bytes 5242896 | tf_op jit(solution)/shard_map/all_gather | solution.py:66
  97.7 22.9 %fusion = (f32[4,320]{1,0:T(4,128)S(1)}, f32[10240,320,4]{0,1,2:T(8,128)}) fusion(pred[320,10240]{1,0:T(8,128)(4,1)} %compare_and_fusion, bf16[10240,256]{1,0:T(8,128)(2,1)} %all-gather.3.cloned.1.call-done, bf16[320,512]{1,0:T(8,128)(2,1)S(1)} %copy-done), kind=kOutput, calls=%fused_computation.4 | convolution fusion | flops 3394763520 | bytes 58659840 | tf_op jit(solution)/shard_map/qgjd,kgd->gjqk/dot_general | solution.py:79
  120.5 22.7 %fusion.1 = f32[4,320]{1,0:T(4,128)S(1)} fusion(f32[10240,320,4]{0,1,2:T(8,128)} %get-tuple-element.14, f32[4,320]{1,0:T(4,128)S(1)} %broadcast_maximum_fusion, pred[320,10240]{1,0:T(8,128)(4,1)} %compare_and_fusion), kind=kLoop, calls=%fused_computation.5 | loop fusion | flops 65534720 | bytes 55715840 | tf_op jit(solution)/shard_map/reduce_sum | solution.py:90
  143.3 23.2 %fusion.20 = bf16[320,1,4,128]{3,0,2,1:T(8,128)(2,1)S(1)} fusion(f32[10240,320,4]{0,1,2:T(8,128)} %get-tuple-element.14, f32[4,320]{1,0:T(4,128)S(1)} %broadcast_maximum_fusion, pred[320,10240]{1,0:T(8,128)(4,1)} %compare_and_fusion, f32[4,320]{1,0:T(4,128)S(1)} %fusion.1, bf16[10240,256]{1,0:T(8,128)(2,1)} %all-gather.3.cloned.1.call-done), kind=kOutput, calls=%fused_computation.20 | convolution fusion | flops 3421306880 | bytes 58664960 | tf_op jit(solution)/shard_map/gjqk,kgd->gjqd/dot_general | solution.py:91
  166.5 0.3 copy.19
  166.8 34.2 %all-gather.5.cloned.1.call-done = bf16[512,8192]{1,0:T(8,128)(2,1)} async-done(((bf16[512,256]{1,0:T(8,128)(2,1)}), bf16[512,8192]{1,0:T(8,128)(2,1)}) %all-gather.5.cloned.1.call-update) | async-done | bytes 8388624 | tf_op jit(solution)/shard_map/all_gather | solution.py:101
  200.9 8.0 %convolution_convert_fusion = bf16[320,8192]{1,0:T(8,128)(2,1)} fusion(bf16[512,8192]{1,0:T(8,128)(2,1)} %all-gather.5.cloned.1.call-done, bf16[40,8,4,128]{3,2,1,0:T(4,128)(2,1)S(1)} %bitcast.67), kind=kOutput, calls=%fused_computation.11 | convolution fusion | flops 2686976000 | bytes 13959168 | tf_op jit(solution)/shard_map/dot_general | solution.py:99
  208.9 3.7 %fusion.62 = (bf16[10240,128]{1,0:T(8,128)(2,1)S(1)}, bf16[10240,128]{1,0:T(8,128)(2,1)}) fusion(bf16[10240,256]{1,0:T(8,128)(2,1)} %all-gather.3.cloned.1.call-done), kind=kLoop, calls=%fused_computation.91 | loop fusion | bytes 10485760 | tf_op jit(solution)/shard_map/slice | solution.py:70
  212.6 3.8 %gather_fusion = bf16[704,128]{1,0:T(8,128)(2,1)S(1)} fusion(bf16[10240,128]{1,0:T(8,128)(2,1)} %get-tuple-element.10, s32[1024]{0:T(1024)S(1)} %pad_clamp_fusion), kind=kCustom, calls=%fused_computation.clone | custom fusion | bytes 363264 | tf_op jit(solution)/shard_map/jit(_take)/gather | solution.py:116
  216.5 2.0 gather_fusion.1
  218.5 1.0 select_select_fusion
  219.5 71.0 %all-reduce.2.cloned.1.call-done = bf16[320,8192]{1,0:T(8,128)(2,1)} async-done(((bf16[320,8192]{1,0:T(8,128)(2,1)}), bf16[320,8192]{1,0:T(8,128)(2,1)}) %all-reduce.2.cloned.1.call-update) | async-done | bytes 5242896 | tf_op jit(solution)/shard_map/psum | solution.py:104
  290.5 6.0 %multiply_reduce_fusion = f32[320]{0:T(512)S(1)} fusion(bf16[320,8192]{1,0:T(8,128)(2,1)} %all-reduce.2.cloned.1.call-done, bf16[320,8192]{1,0:T(8,128)(2,1)} %param.13), kind=kLoop, calls=%fused_computation.13 | loop fusion | flops 13106880 | bytes 10487040 | tf_op jit(solution)/shard_map/reduce_sum | solution.py:106
  296.5 7.1 %multiply_convert_fusion = bf16[320,8192]{1,0:T(8,128)(2,1)} fusion(bf16[320,8192]{1,0:T(8,128)(2,1)S(1)} %copy-done.2, bf16[320,8192]{1,0:T(8,128)(2,1)} %param.13, f32[8192]{0:T(1024)S(1)} %convert_element_type.52, f32[320]{0:T(512)S(1)} %add_rsqrt_fusion), kind=kLoop, calls=%fused_computation.12 | loop fusion | flops 15728640 | bytes 15762688 | tf_op jit(solution)/shard_map/convert_element_type | solution.py:107
  (18 shorter events, 0.2 us)
Async XLA Ops:
  7.2 90.5 %copy-start = (bf16[320,512]{1,0:T(8,128)(2,1)S(1)}, bf16[320,512]{1,0:T(8,128)(2,1)}, u32[]{:S(2)}) copy-start(bf16[320,512]{1,0:T(8,128)(2,1)} %param.9) | copy-start | bytes 983044
  7.2 90.5 %all-gather.3.cloned.1.call-start = ((), (), s32[]{:S(2)}) async-start(), calls=%async_computation | async-start | bytes 5406720 | tf_op jit(solution)/shard_map/all_gather | solution.py:66
  8.9 192.0 %all-gather.5.cloned.1.call-start = ((), (), s32[]{:S(2)}) async-start(), calls=%async_computation.1 | async-start | bytes 8650752 | tf_op jit(solution)/shard_map/all_gather | solution.py:101
  9.7 280.8 %all-reduce.2.cloned.1.call-start = ((), (), s32[]{:S(2)}) async-start(), calls=%async_computation.2 | async-start | bytes 10485760 | tf_op jit(solution)/shard_map/psum | solution.py:104
  290.5 6.0 %copy-start.2 = (bf16[320,8192]{1,0:T(8,128)(2,1)S(1)}, bf16[320,8192]{1,0:T(8,128)(2,1)}, u32[]{:S(2)}) copy-start(bf16[320,8192]{1,0:T(8,128)(2,1)} %all-reduce.2.cloned.1.call-done) | copy-start | bytes 15728644
  290.5 13.1 %copy-start.1 = (bf16[320,512]{1,0:T(8,128)(2,1)S(1)}, bf16[320,512]{1,0:T(8,128)(2,1)}, u32[]{:S(2)}) copy-start(bf16[320,512]{1,0:T(8,128)(2,1)} %param.9) | copy-start | bytes 983044
Sparse Core Ops, SparseCore 0:
  11.2 86.4 all-gather.2
  100.1 100.7 all-gather.4
  209.0 81.3 all-reduce.1
where the time goes:
time: 310 us
  waiting for transfers between devices  184 us (59%)
  matrix products  54.1 us (17%)
  other arithmetic  47.3 us (15%)
  between operations  13.9 us (4%)
  local copies, waits for them, and re-layouts  10.7 us (3%)
    all_gather x1, waiting for transfers between devices, body(): lax.all_gather(jnp.concatenate([key_rows, value_rows], axis=1), 'seq', ax...  78.3 us
    psum x1, waiting for transfers between devices, body(): lax.psum(partial_value.astype(jnp.bfloat16), 'tensor').astype(jnp.float32)  71 us
    all_gather x1, waiting for transfers between devices, body(): lax.all_gather(out_weight, 'seq', axis=1, tiled=True)  34.2 us
    dot_general x1, matrix products, body(): jnp.einsum('gjqk,kgd->gjqd', weights.astype(jnp.bfloat16), value_piece.re...  23.2 us
    dot_general x1, matrix products, body(): jnp.einsum('qgjd,kgd->gjqk', grouped, key_piece.reshape(piece_rows, kv_lo...  22.9 us
    reduce_sum x1, other arithmetic, body(): total_new = jnp.sum(weights, axis=-1)  22.7 us
    dot_general x1, matrix products, body(): jnp.dot(attended, lax.all_gather(out_weight, 'seq', axis=1, tiled=True),...  7.96 us
    convert_element_type x1, other arithmetic, body(): (hidden * lax.rsqrt(mean_square + 1e-05) * norm_gain.astype(jnp.float32))...  7.13 us
  transfers between devices with their start and end apart: 3, of which 3 were waited for; matrix products, arithmetic and copies ran while one was open for 29% of the time, Pallas kernels for 0%

commit v1 on v0

--- a/solution.py
+++ b/solution.py
@@ -101,7 +101,9 @@
         lax.all_gather(out_weight, "seq", axis=1, tiled=True),
         preferred_element_type=jnp.float32,
     )
-    projected = lax.psum(partial_value.astype(jnp.bfloat16), "tensor").astype(jnp.float32)
+    projected = jnp.sum(
+        lax.all_gather(partial_value.astype(jnp.bfloat16), "tensor"), axis=0
+    ).astype(jnp.float32)
     hidden = residual_in.astype(jnp.float32) + projected
     mean_square = jnp.mean(hidden * hidden, axis=-1, keepdims=True)
     normed = (hidden * lax.rsqrt(mean_square + 1e-05) * norm_gain.astype(jnp.float32)).astype(

time: 310 us -> 442 us (1.43)
  waiting for transfers between devices: 184 us -> 302 us
  other arithmetic: 47.3 us -> 61 us
    all_gather x0 -> x1, waiting for transfers between devices: none -> 185 us  [body(): lax.all_gather(partial_value.astype(jnp.bfloat16), 'tensor')]
    psum x1 -> x0, waiting for transfers between devices: 71 us -> none  [body(): lax.psum(partial_value.astype(jnp.bfloat16), 'tensor').astype(jnp.float32)]
    reduce_sum x0 -> x1, other arithmetic: none -> 17.1 us  [body(): jnp.sum(lax.all_gather(partial_value.astype(jnp.bfloat16), 'tensor'), axi...]
  transfers between devices with their start and end apart: 3 -> 3, of which waited for: 3 -> 3; matrix products, arithmetic and copies ran while one was open for 29% -> 19% of each run, Pallas kernels for 0% -> 0%
where the time goes in v1:
time: 442 us; the launch traced here: 441 us
  waiting for transfers between devices  302 us (68%)
  other arithmetic  61 us (14%)
  matrix products  54.1 us (12%)
  between operations  13.9 us (3%)
  local copies, waits for them, and re-layouts  10.8 us (2%)
    all_gather x1, waiting for transfers between devices, body(): lax.all_gather(partial_value.astype(jnp.bfloat16), 'tensor')  185 us
    all_gather x1, waiting for transfers between devices, body(): lax.all_gather(jnp.concatenate([key_rows, value_rows], axis=1), 'seq', ax...  82.1 us
    all_gather x1, waiting for transfers between devices, body(): lax.all_gather(out_weight, 'seq', axis=1, tiled=True)  34.1 us
    dot_general x1, matrix products, body(): jnp.einsum('gjqk,kgd->gjqd', weights.astype(jnp.bfloat16), value_piece.re...  23.2 us
    dot_general x1, matrix products, body(): jnp.einsum('qgjd,kgd->gjqk', grouped, key_piece.reshape(piece_rows, kv_lo...  22.9 us
    reduce_sum x1, other arithmetic, body(): total_new = jnp.sum(weights, axis=-1)  22.7 us
    reduce_sum x1, other arithmetic, body(): jnp.sum(lax.all_gather(partial_value.astype(jnp.bfloat16), 'tensor'), axi...  17.1 us
  transfers between devices with their start and end apart: 3, of which 3 were waited for; matrix products, arithmetic and copies ran while one was open for 19% of the time, Pallas kernels for 0%

profile of v1, /device:TPU:1, one launch (start us, length us, event | category | flops | bytes accessed | tf_op | source)
XLA Modules:
  0.0 441.4 jit_solution(9128006849882406276)
XLA Ops:
  7.2 0.0 copy-start
  7.2 0.0 all-gather.5.cloned.1.call-start
  7.2 1.6 pad_maximum_fusion
  8.9 0.0 all-gather.5.cloned.1.call-update
  8.9 0.0 all-gather.7.cloned.1.call-start
  9.0 0.7 all-gather.7.cloned.1.call-update
  9.7 0.0 all-gather.9.cloned.1.call-start
  9.7 0.7 copy.17
  10.5 0.1 reduce.3
  10.6 0.1 convert_reduce_fusion.1
  10.8 0.2 convert_reduce_fusion
  11.0 4.6 %compare_and_fusion = pred[320,10240]{1,0:T(8,128)(4,1)} fusion(s32[10240]{0:T(1024)S(1)} %convert_reduce_fusion, s32[10240]{0:T(1024)S(1)} %fusion.43, s32[320]{0:T(512)S(1)} %convert_reduce_fusion.1, s32[320]{0:T(512)S(1)} %add_select_fusion.5), kind=kLoop, calls=%fused_computation.10 | loop fusion | flops 9830400 | bytes 3361280 | tf_op jit(solution)/shard_map/and | solution.py:74
  15.6 82.1 %all-gather.5.cloned.1.call-done = bf16[10240,256]{1,0:T(8,128)(2,1)} async-done(((bf16[320,256]{1,0:T(8,128)(2,1)}), bf16[10240,256]{1,0:T(8,128)(2,1)}) %all-gather.5.cloned.1.call-update) | async-done | bytes 5242896 | tf_op jit(solution)/shard_map/all_gather | solution.py:66
  97.7 22.9 %fusion = (f32[4,320]{1,0:T(4,128)S(1)}, f32[10240,320,4]{0,1,2:T(8,128)}) fusion(pred[320,10240]{1,0:T(8,128)(4,1)} %compare_and_fusion, bf16[10240,256]{1,0:T(8,128)(2,1)} %all-gather.5.cloned.1.call-done, bf16[320,512]{1,0:T(8,128)(2,1)S(1)} %copy-done), kind=kOutput, calls=%fused_computation.4 | convolution fusion | flops 3394763520 | bytes 58659840 | tf_op jit(solution)/shard_map/qgjd,kgd->gjqk/dot_general | solution.py:79
  120.5 22.7 %fusion.1 = f32[4,320]{1,0:T(4,128)S(1)} fusion(f32[10240,320,4]{0,1,2:T(8,128)} %get-tuple-element.14, f32[4,320]{1,0:T(4,128)S(1)} %broadcast_maximum_fusion, pred[320,10240]{1,0:T(8,128)(4,1)} %compare_and_fusion), kind=kLoop, calls=%fused_computation.5 | loop fusion | flops 65534720 | bytes 55715840 | tf_op jit(solution)/shard_map/reduce_sum | solution.py:90
  143.3 23.2 %fusion.20 = bf16[320,1,4,128]{3,0,2,1:T(8,128)(2,1)S(1)} fusion(f32[10240,320,4]{0,1,2:T(8,128)} %get-tuple-element.14, f32[4,320]{1,0:T(4,128)S(1)} %broadcast_maximum_fusion, pred[320,10240]{1,0:T(8,128)(4,1)} %compare_and_fusion, f32[4,320]{1,0:T(4,128)S(1)} %fusion.1, bf16[10240,256]{1,0:T(8,128)(2,1)} %all-gather.5.cloned.1.call-done), kind=kOutput, calls=%fused_computation.20 | convolution fusion | flops 3421306880 | bytes 58664960 | tf_op jit(solution)/shard_map/gjqk,kgd->gjqd/dot_general | solution.py:91
  166.5 0.3 copy.19
  166.8 0.0 copy-start.4
  166.8 34.1 %all-gather.7.cloned.1.call-done = bf16[512,8192]{1,0:T(8,128)(2,1)} async-done(((bf16[512,256]{1,0:T(8,128)(2,1)}), bf16[512,8192]{1,0:T(8,128)(2,1)}) %all-gather.7.cloned.1.call-update) | async-done | bytes 8388624 | tf_op jit(solution)/shard_map/all_gather | solution.py:101
  200.9 8.0 %convolution_convert_fusion = bf16[320,8192]{1,0:T(8,128)(2,1)} fusion(bf16[512,8192]{1,0:T(8,128)(2,1)} %all-gather.7.cloned.1.call-done, bf16[40,8,4,128]{3,2,1,0:T(4,128)(2,1)S(1)} %bitcast.69), kind=kOutput, calls=%fused_computation.11 | convolution fusion | flops 2686976000 | bytes 13959168 | tf_op jit(solution)/shard_map/dot_general | solution.py:99
  208.9 0.0 all-gather.9.cloned.1.call-update
  208.9 0.1 copy.20
  209.1 0.1 reduce.4
  209.2 0.1 fusion.36
  209.4 3.8 fusion.62
  213.2 3.8 gather_fusion
  217.1 2.0 gather_fusion.1
  219.1 1.0 select_select_fusion
  220.1 184.6 %all-gather.9.cloned.1.call-done = bf16[2560,8192]{1,0:T(8,128)(2,1)} async-done(((bf16[320,8192]{1,0:T(8,128)(2,1)}), bf16[2560,8192]{1,0:T(8,128)(2,1)}) %all-gather.9.cloned.1.call-update) | async-done | bytes 41943056 | tf_op jit(solution)/shard_map/all_gather | solution.py:105
  404.7 17.1 %reduce_sum.78 = bf16[320,8192]{1,0:T(8,128)(2,1)} reduce(bf16[8,320,8192]{2,1,0:T(8,128)(2,1)} %bitcast.68, bf16[]{:T(256)} %constant.116.clone.1), dimensions={0}, to_apply=%region_5.6 | reduce | flops 18350080 | bytes 47185920 | tf_op jit(solution)/shard_map/reduce_sum | solution.py:104
  421.8 6.0 %multiply_reduce_fusion = f32[320]{0:T(512)S(1)} fusion(bf16[320,8192]{1,0:T(8,128)(2,1)} %reduce_sum.78, bf16[320,8192]{1,0:T(8,128)(2,1)} %param.13), kind=kLoop, calls=%fused_computation.13 | loop fusion | flops 13106880 | bytes 10487040 | tf_op jit(solution)/shard_map/reduce_sum | solution.py:108
  427.8 7.1 %multiply_convert_fusion = bf16[320,8192]{1,0:T(8,128)(2,1)} fusion(bf16[320,8192]{1,0:T(8,128)(2,1)S(1)} %copy-done.2, bf16[320,8192]{1,0:T(8,128)(2,1)} %param.13, f32[8192]{0:T(1024)S(1)} %convert_element_type.54, f32[320]{0:T(512)S(1)} %add_rsqrt_fusion), kind=kLoop, calls=%fused_computation.12 | loop fusion | flops 15728640 | bytes 15762688 | tf_op jit(solution)/shard_map/convert_element_type | solution.py:109
  (23 shorter events, 0.3 us)
Async XLA Ops:
  7.2 90.5 %copy-start = (bf16[320,512]{1,0:T(8,128)(2,1)S(1)}, bf16[320,512]{1,0:T(8,128)(2,1)}, u32[]{:S(2)}) copy-start(bf16[320,512]{1,0:T(8,128)(2,1)} %param.9) | copy-start | bytes 983044
  7.2 90.5 %all-gather.5.cloned.1.call-start = ((), (), s32[]{:S(2)}) async-start(), calls=%async_computation | async-start | bytes 5406720 | tf_op jit(solution)/shard_map/all_gather | solution.py:66
  8.9 192.0 %all-gather.7.cloned.1.call-start = ((), (), s32[]{:S(2)}) async-start(), calls=%async_computation.1 | async-start | bytes 8650752 | tf_op jit(solution)/shard_map/all_gather | solution.py:101
  9.7 395.0 %all-gather.9.cloned.1.call-start = ((), (), s32[]{:S(2)}) async-start(), calls=%async_computation.2 | async-start | bytes 47185920 | tf_op jit(solution)/shard_map/all_gather | solution.py:105
  166.8 42.1 %copy-start.3 = (bf16[8192]{0:T(1024)(128)(2,1)S(1)}, bf16[8192]{0:T(1024)(128)(2,1)}, u32[]{:S(2)}) copy-start(bf16[8192]{0:T(1024)(128)(2,1)} %param.14) | copy-start | bytes 49156
  166.8 42.2 %copy-start.4 = (s32[18]{0:T(128)S(1)}, s32[18]{0:T(128)}, u32[]{:S(2)}) copy-start(s32[18]{0:T(128)} %param.15) | copy-start | bytes 220
  421.8 6.0 %copy-start.2 = (bf16[320,8192]{1,0:T(8,128)(2,1)S(1)}, bf16[320,8192]{1,0:T(8,128)(2,1)}, u32[]{:S(2)}) copy-start(bf16[320,8192]{1,0:T(8,128)(2,1)} %reduce_sum.78) | copy-start | bytes 15728644
  421.8 13.1 %copy-start.1 = (bf16[320,512]{1,0:T(8,128)(2,1)S(1)}, bf16[320,512]{1,0:T(8,128)(2,1)}, u32[]{:S(2)}) copy-start(bf16[320,512]{1,0:T(8,128)(2,1)} %param.9) | copy-start | bytes 983044
Sparse Core Ops, SparseCore 0:
  11.2 86.4 all-gather.4
  100.1 100.7 all-gather.6
  209.0 195.5 all-gather.8
